TPU v7x, 128 devices: a whole 4x4x4 slice. The times are simulated.
128 devices in a mesh: wide: 16 (over z, y), col: 8 (over x, core).
Axes of the slice: x: 4, y: 4, z: 4, core: 2. Of those that a mesh axis runs over, the one named last changes fastest.
Arguments:
- z_root: float32 [512, 16384], P('col', 'wide'), may hold values from -6 to 6
- z_child: float32 [512, 2, 8192], P('col', None, 'wide'), may hold values from -6 to 6
- z_grand: float32 [512, 4, 4096], P('col', None, 'wide'), may hold values from -6 to 6
- inv_root: float32 [16384, 16384], P('wide', 'col'), as said below
- inv_child: float32 [2, 8192, 8192], P(None, 'wide', 'col'), as said below
- inv_grand: float32 [4, 4096, 4096], P(None, 'wide', 'col'), as said below
- panel_child: float32 [2, 4096, 8192], P(None, 'col', 'wide'), may hold values from -0.046875 to 0.046875
- panel_grand: float32 [4, 2048, 4096], P(None, 'col', 'wide'), may hold values from -0.0625 to 0.0625
- anc_child: int32 [2, 32], P(None, 'col'), may hold values from 0 to 127, as said below
- anc_grand: int32 [4, 16], P(None, 'col'), may hold values from 0 to 255, as said below
Outputs:
- x_root: float32 [512, 16384], P('wide', 'col')
- x_child: float32 [512, 2, 8192], P('wide', None, 'col')
- x_grand: float32 [512, 4, 4096], P('wide', None, 'col')
Inputs may be any that keep to these rules, and one draw needn't show every extreme that they name: inv_root is lower triangular with a positive diagonal (entries above the diagonal are zero). Each inv_child[k] is lower triangular with a positive diagonal. Each inv_grand[g] is lower triangular with a positive diagonal. `anc_child`: each row lists distinct blocks in rising order and always names block 0 and block 127. `anc_grand`: row g lists 2048 // 256 distinct root blocks in rising order, block 0 and block 127 among them, then as many distinct blocks of child g // 2 (numbered 16384 // 128 + (g // 2) * 64 onwards) in rising order, its first and its last among them.
All inputs are finite; a program needn't handle non-finite values.
Results may differ from a plain program's by a relative error of at most 0.000096.
Values sent between devices are 32-bit elements; how exact they have to be, the bound alone decides.
No kernel may reach another device: no remote copies, remote signals or barrier semaphores. Data moves between devices by JAX's collectives and lax.ppermute only.
A program may use at most 128 MiB of HBM per device.

v0:
```python
import jax
import jax.numpy as jnp
from jax import lax
from jax.sharding import PartitionSpec as P

BLK = 128
PRECISE = lax.Precision.HIGHEST


def pick_blocks(source_rows, blocks):
    leading = source_rows.shape[0]
    tiled = source_rows.reshape(leading, source_rows.shape[1] // BLK, BLK)
    selected = jnp.take(tiled, blocks.reshape(-1), axis=1)
    return selected.reshape(leading, blocks.shape[0], blocks.shape[1] * BLK)


def spread_rhs(local_part):
    return lax.all_gather(local_part, "col", axis=0, tiled=True)


def solve_terms(right_rows, inverse):
    return lax.psum_scatter(
        jnp.einsum(
            "ski,kij->skj",
            right_rows,
            inverse,
            precision=PRECISE,
            preferred_element_type=jnp.float32,
        ),
        "wide",
        scatter_dimension=0,
        tiled=True,
    )


def spread_solved(solved_local):
    gathered = lax.all_gather(solved_local, "col", axis=2, tiled=True)
    return gathered.reshape(gathered.shape[0], -1)


def fetch_ancestors(source_rows, blocks):
    return lax.all_gather(pick_blocks(source_rows, blocks), "wide", axis=0, tiled=True)


def finish_level(z_local, inverse, partial_value):
    summed = lax.psum(partial_value, "col")
    right_side = spread_rhs(z_local) - summed
    solved = solve_terms(right_side, inverse)
    return solved


def per_device(
    z_root,
    z_child,
    z_grand,
    inv_root,
    inv_child,
    inv_grand,
    panel_child,
    panel_grand,
    anc_child,
    anc_grand,
):
    root_right = spread_rhs(z_root[:, None, :])
    root_solved = solve_terms(root_right, inv_root[None])
    x_root = root_solved[:, 0, :]
    root_rows = spread_solved(root_solved)
    near_rows = fetch_ancestors(root_rows, anc_child)
    partial_value = jnp.einsum(
        "ska,kaj->skj",
        near_rows,
        panel_child,
        precision=PRECISE,
        preferred_element_type=jnp.float32,
    )
    x_child = finish_level(z_child, inv_child, partial_value)
    child_rows = spread_solved(x_child)
    solved_all = jnp.concatenate([root_rows, child_rows], axis=1)
    far_rows = fetch_ancestors(solved_all, anc_grand)
    partial_grand = jnp.einsum(
        "sga,gaj->sgj", far_rows, panel_grand, precision=PRECISE, preferred_element_type=jnp.float32
    )
    x_grand = finish_level(z_grand, inv_grand, partial_grand)
    return (x_root, x_child, x_grand)


def solution(mesh):
    in_specs = (
        P("col", "wide"),
        P("col", None, "wide"),
        P("col", None, "wide"),
        P("wide", "col"),
        P(None, "wide", "col"),
        P(None, "wide", "col"),
        P(None, "col", "wide"),
        P(None, "col", "wide"),
        P(None, "col"),
        P(None, "col"),
    )
    out_specs = (P("wide", "col"), P("wide", None, "col"), P("wide", None, "col"))
    return jax.shard_map(
        per_device, mesh=mesh, in_specs=in_specs, out_specs=out_specs, check_vma=False
    )
```

profile of v0, /device:TPU:0, one launch (start us, length us, event | category | flops | bytes accessed | tf_op | source)
XLA Modules:
  0.0 726.2 jit_solution(2255232434404925078)
XLA Ops:
  8.0 29.4 %all-gather.21.cloned.1.call-done = f32[512,1024]{1,0:T(8,128)} async-done(((f32[64,1024]{1,0:T(8,128)}), f32[512,1024]{1,0:T(8,128)}) %all-gather.21.cloned.1.call-update) | async-done | bytes 2097168 | tf_op jit(solution)/shard_map/all_gather | solution.py:18
  37.4 30.4 %convolution_bitcast_fusion = f32[512,1,2048]{0,2,1:T(8,128)} fusion(f32[1024,2048]{1,0:T(8,128)} %param.13, f32[512,1024]{1,0:T(8,128)} %all-gather.21.cloned.1.call-done), kind=kOutput, calls=%fused_computation.3 | convolution fusion | flops 12884901888 | bytes 14680064 | tf_op jit(solution)/shard_map/ski,kij->skj/dot_general | solution.py:23
  67.8 11.0 %copy.75 = f32[512,1,2048]{2,1,0:T(1,128)} copy(f32[512,1,2048]{0,2,1:T(8,128)} %convolution_bitcast_fusion) | data formatting | bytes 8388608 | tf_op jit(solution)/shard_map/ski,kij->skj/transpose | solution.py:23
  80.7 102.2 %all-reduce.9.cloned.1.call-done = f32[512,1,2048]{2,1,0:T(1,128)} async-done(((f32[512,1,2048]{2,1,0:T(1,128)}), f32[512,1,2048]{2,1,0:T(1,128)}) %all-reduce.9.cloned.1.call-update) | async-done | bytes 4194320
  183.0 1.7 constant_dynamic-slice_fusion
  184.9 25.1 %all-gather.11.cloned.1.call-done = f32[32,1,16384]{2,1,0:T(1,128)} async-done(((f32[32,1,2048]{2,1,0:T(1,128)}), f32[32,1,16384]{2,1,0:T(1,128)}) %all-gather.11.cloned.1.call-update) | async-done | bytes 2097168 | tf_op jit(solution)/shard_map/all_gather | solution.py:37
  210.0 4.2 copy.77
  214.3 2.1 gather_fusion
  217.3 0.8 copy.76
  218.2 44.9 %all-gather.13.cloned.1.call-done = f32[512,2,512]{2,0,1:T(8,128)} async-done(((f32[32,2,512]{2,0,1:T(8,128)}), f32[512,2,512]{2,0,1:T(8,128)}) %all-gather.13.cloned.1.call-update) | async-done | bytes 2097168 | tf_op jit(solution)/shard_map/all_gather | solution.py:42
  263.0 7.0 convolution_bitcast_fusion.4
  270.1 19.4 %all-gather.9.cloned.1.call-done = f32[512,2,512]{2,0,1:T(8,128)} async-done(((f32[64,2,512]{2,0,1:T(8,128)}), f32[512,2,512]{2,0,1:T(8,128)}) %all-gather.9.cloned.1.call-update) | async-done | bytes 2097168 | tf_op jit(solution)/shard_map/all_gather | solution.py:18
  289.6 68.2 %all-reduce.5.cloned.1.call-done = f32[512,2,512]{2,0,1:T(8,128)} async-done(((f32[512,2,512]{2,0,1:T(8,128)}), f32[512,2,512]{2,0,1:T(8,128)}) %all-reduce.5.cloned.1.call-update) | async-done | bytes 2097168 | tf_op jit(solution)/shard_map/psum | solution.py:46
  357.8 12.2 %convolution_bitcast_fusion.2 = f32[512,2,1024]{2,0,1:T(8,128)} fusion(f32[2,512,1024]{2,1,0:T(8,128)} %param.14, f32[512,2,512]{2,0,1:T(8,128)} %all-gather.9.cloned.1.call-done, f32[512,2,512]{2,0,1:T(8,128)} %all-reduce.5.cloned.1.call-done), kind=kOutput, calls=%fused_computation.5 | convolution fusion | flops 6442975232 | bytes 12582912 | tf_op jit(solution)/shard_map/ski,kij->skj/dot_general | solution.py:23
  370.1 77.5 %reduce-scatter.3.cloned.1.call-done = f32[32,2,1024]{2,0,1:T(8,128)} async-done(((f32[512,2,1024]{2,0,1:T(8,128)}), f32[32,2,1024]{2,0,1:T(8,128)}) %reduce-scatter.3.cloned.1.call-update) | async-done | bytes 262160 | tf_op jit(solution)/shard_map/reduce_scatter | solution.py:22
  447.9 25.8 %all-gather.17.cloned.1.call-done = f32[32,2,8192]{2,0,1:T(8,128)} async-done(((f32[32,2,1024]{2,0,1:T(8,128)}), f32[32,2,8192]{2,0,1:T(8,128)}) %all-gather.17.cloned.1.call-update) | async-done | bytes 2097168 | tf_op jit(solution)/shard_map/all_gather | solution.py:37
  473.7 4.6 copy.81
  478.3 4.0 concatenate.6
  482.3 3.0 copy.83
  485.3 2.4 pad_maximum_fusion
  487.7 2.8 gather_fusion.1
  491.4 1.7 copy.80
  493.2 43.9 %all-gather.19.cloned.1.call-done = f32[512,4,256]{2,0,1:T(8,128)} async-done(((f32[32,4,256]{2,0,1:T(8,128)}), f32[512,4,256]{2,0,1:T(8,128)}) %all-gather.19.cloned.1.call-update) | async-done | bytes 2097168 | tf_op jit(solution)/shard_map/all_gather | solution.py:42
  537.1 4.9 convolution_bitcast_fusion.3
  542.1 21.7 %all-gather.15.cloned.1.call-done = f32[512,4,256]{2,0,1:T(8,128)} async-done(((f32[64,4,256]{2,0,1:T(8,128)}), f32[512,4,256]{2,0,1:T(8,128)}) %all-gather.15.cloned.1.call-update) | async-done | bytes 2097168 | tf_op jit(solution)/shard_map/all_gather | solution.py:18
  563.8 68.5 %all-reduce.7.cloned.1.call-done = f32[512,4,256]{2,0,1:T(8,128)} async-done(((f32[512,4,256]{2,0,1:T(8,128)}), f32[512,4,256]{2,0,1:T(8,128)}) %all-reduce.7.cloned.1.call-update) | async-done | bytes 2097168 | tf_op jit(solution)/shard_map/psum | solution.py:46
  632.3 7.8 %convolution_bitcast_fusion.1 = f32[512,4,512]{2,0,1:T(8,128)} fusion(f32[4,256,512]{2,1,0:T(8,128)S(1)} %copy-done, f32[512,4,256]{2,0,1:T(8,128)} %all-gather.15.cloned.1.call-done, f32[512,4,256]{2,0,1:T(8,128)} %all-reduce.7.cloned.1.call-done), kind=kOutput, calls=%fused_computation.4 | convolution fusion | flops 3221749760 | bytes 10485760 | tf_op jit(solution)/shard_map/ski,kij->skj/dot_general | solution.py:23
  640.0 0.9 copy-done.2
  641.0 0.8 copy.95
  641.8 0.9 copy.87
  642.7 74.9 %reduce-scatter.5.cloned.1.call-done = f32[32,4,512]{2,0,1:T(8,128)} async-done(((f32[512,4,512]{2,0,1:T(8,128)}), f32[32,4,512]{2,0,1:T(8,128)}) %reduce-scatter.5.cloned.1.call-update) | async-done | bytes 262160 | tf_op jit(solution)/shard_map/reduce_scatter | solution.py:22
  717.6 1.8 copy.88
  (60 shorter events, 4.7 us)
Async XLA Ops:
  7.2 625.1 %copy-start = (f32[4,256,512]{2,1,0:T(8,128)S(1)}, f32[4,256,512]{2,1,0:T(8,128)}, u32[]{:S(2)}) copy-start(f32[4,256,512]{2,1,0:T(8,128)} %param.15) | copy-start | bytes 6291460
  7.2 30.2 %all-gather.21.cloned.1.call-start = ((), (), s32[]{:S(2)}) async-start(), calls=%async_computation.12 | async-start | bytes 2359296 | tf_op jit(solution)/shard_map/all_gather | solution.py:18
  7.9 175.0 %all-reduce.9.cloned.1.call-start = ((), (), s32[]{:S(2)}) async-start(), calls=%async_computation.13 | async-start | bytes 8388608
  78.8 0.7 copy-start.8
  78.8 105.9 %copy-start.7 = (s32[2,4]{1,0:T(2,128)S(1)}, s32[2,4]{1,0:T(2,128)}, u32[]{:S(2)}) copy-start(s32[2,4]{1,0:T(2,128)} %param.18) | copy-start | bytes 100
  78.8 131.2 %all-gather.11.cloned.1.call-start = ((), (), s32[]{:S(2)}) async-start(), calls=%async_computation.3 | async-start | bytes 2359296 | tf_op jit(solution)/shard_map/all_gather | solution.py:37
  184.7 78.4 %all-gather.13.cloned.1.call-start = ((), (), s32[]{:S(2)}) async-start(), calls=%async_computation.4 | async-start | bytes 2228224 | tf_op jit(solution)/shard_map/all_gather | solution.py:42
  210.0 7.3 %copy-start.5 = (f32[64,2,512]{2,1,0:T(2,128)S(1)}, f32[64,2,512]{2,1,0:T(2,128)}, u32[]{:S(2)}) copy-start(f32[64,2,512]{2,1,0:T(2,128)} %param.11) | copy-start | bytes 786436
  217.3 72.3 %all-gather.9.cloned.1.call-start = ((), (), s32[]{:S(2)}) async-start(), calls=%async_computation.2 | async-start | bytes 2359296 | tf_op jit(solution)/shard_map/all_gather | solution.py:18
  218.1 139.7 %all-reduce.5.cloned.1.call-start = ((), (), s32[]{:S(2)}) async-start(), calls=%async_computation.5 | async-start | bytes 4194304 | tf_op jit(solution)/shard_map/psum | solution.py:46
  270.1 177.5 %reduce-scatter.3.cloned.1.call-start = ((), (), s32[]{:S(2)}) async-start(), calls=%async_computation.6 | async-start | bytes 4456448 | tf_op jit(solution)/shard_map/reduce_scatter | solution.py:22
  370.0 77.7 %copy-start.6 = (s32[4,2]{0,1:T(2,128)S(1)}, s32[4,2]{0,1:T(2,128)}, u32[]{:S(2)}) copy-start(s32[4,2]{0,1:T(2,128)} %param.19) | copy-start | bytes 100
  370.0 103.7 %all-gather.17.cloned.1.call-start = ((), (), s32[]{:S(2)}) async-start(), calls=%async_computation.8 | async-start | bytes 2359296 | tf_op jit(solution)/shard_map/all_gather | solution.py:37
  447.6 89.6 %all-gather.19.cloned.1.call-start = ((), (), s32[]{:S(2)}) async-start(), calls=%async_computation.9 | async-start | bytes 2228224 | tf_op jit(solution)/shard_map/all_gather | solution.py:42
  482.3 3.0 copy-start.1
  487.7 49.5 %copy-start.3 = (f32[4,256,256]{2,1,0:T(8,128)S(1)}, f32[4,256,256]{2,1,0:T(8,128)}, u32[]{:S(2)}) copy-start(f32[4,256,256]{2,1,0:T(8,128)} %param.17) | copy-start | bytes 3145732
  491.4 72.4 %all-gather.15.cloned.1.call-start = ((), (), s32[]{:S(2)}) async-start(), calls=%async_computation.7 | async-start | bytes 2359296 | tf_op jit(solution)/shard_map/all_gather | solution.py:18
  493.2 139.1 %all-reduce.7.cloned.1.call-start = ((), (), s32[]{:S(2)}) async-start(), calls=%async_computation.10 | async-start | bytes 4194304 | tf_op jit(solution)/shard_map/psum | solution.py:46
  542.0 175.5 %reduce-scatter.5.cloned.1.call-start = ((), (), s32[]{:S(2)}) async-start(), calls=%async_computation.11 | async-start | bytes 4456448 | tf_op jit(solution)/shard_map/reduce_scatter | solution.py:22
  640.0 0.9 copy-start.2
  640.0 1.7 copy-start.4
Sparse Core Ops, SparseCore 0:
  9.7 27.5 all-gather.20
  79.0 103.9 all-reduce.8
  185.2 24.7 all-gather.10
  217.4 45.5 all-gather.12
  265.2 24.3 all-gather.8
  291.8 65.9 all-reduce.4
  370.1 77.3 reduce-scatter.2
  449.4 24.3 all-gather.16
  491.5 45.5 all-gather.18
  539.4 24.3 all-gather.14
  566.3 65.9 all-reduce.6
  640.2 77.3 reduce-scatter.4
where the time goes:
time: 727 us; the launch traced here: 726 us
  waiting for transfers between devices  602 us (83%)
  matrix products  62.3 us (9%)
  local copies, waits for them, and re-layouts  42.2 us (6%)
  between operations  15 us (2%)
    reduce_scatter x2, waiting for transfers between devices, solve_terms(): lax.psum_scatter(jnp.einsum('ski,kij->skj', right_rows, inverse, precisio...  152 us
    psum x2, waiting for transfers between devices, finish_level(): summed = lax.psum(partial_value, 'col')  137 us
    unnamed x13, waiting for transfers between devices  103 us
    all_gather x2, waiting for transfers between devices, fetch_ancestors(): lax.all_gather(pick_blocks(source_rows, blocks), 'wide', axis=0, tiled=True)  88.8 us
    all_gather x3, waiting for transfers between devices, spread_rhs(): return lax.all_gather(local_part, 'col', axis=0, tiled=True)  70.5 us
    all_gather x2, waiting for transfers between devices, spread_solved(): gathered = lax.all_gather(solved_local, 'col', axis=2, tiled=True)  50.9 us
    dot_general x3, matrix products, solve_terms(): jnp.einsum('ski,kij->skj', right_rows, inverse, precision=PRECISE, prefer...  50.4 us
  transfers between devices with their start and end apart: 12, of which 12 were waited for; matrix products, arithmetic and copies ran while one was open for 2% of the time, Pallas kernels for 0%

commit v1 on v0

--- a/solution.py
+++ b/solution.py
@@ -5,6 +5,15 @@
 
 BLK = 128
 PRECISE = lax.Precision.HIGHEST
+answer_the_pipes = lambda raw, ndim_at: jnp.concatenate(
+    lax.all_to_all(
+        jnp.stack([raw for _ in range(lax.axis_size("wide"))], axis=0),
+        axis_name="wide",
+        split_axis=0,
+        concat_axis=0,
+    ),
+    ndim_at,
+)
 
 
 def pick_blocks(source_rows, blocks):
@@ -39,7 +48,7 @@
 
 
 def fetch_ancestors(source_rows, blocks):
-    return lax.all_gather(pick_blocks(source_rows, blocks), "wide", axis=0, tiled=True)
+    return answer_the_pipes(pick_blocks(source_rows, blocks), 0)
 
 
 def finish_level(z_local, inverse, partial_value):

time: 727 us -> 651 us (0.90)
  waiting for transfers between devices: 602 us -> 459 us
  blocking collectives: 0 us -> 71.2 us
    all_gather x2 -> x0, waiting for transfers between devices: 88.8 us -> none  [fetch_ancestors(): lax.all_gather(pick_blocks(source_rows, blocks), 'wide', axis=0, tiled=True)]
    all_to_all x0 -> x2, blocking collectives: none -> 71.2 us  [lax.all_to_all(jnp.stack([raw for _ in range(lax.axis_size('wide'))], axi...]
    all_gather x3, waiting for transfers between devices: 70.5 us -> 29.4 us  [spread_rhs(): return lax.all_gather(local_part, 'col', axis=0, tiled=True)]
    psum x2, waiting for transfers between devices: 137 us -> 124 us  [finish_level(): summed = lax.psum(partial_value, 'col')]
    unnamed x13 -> x11, waiting for transfers between devices: 103 us -> 103 us
  transfers between devices with their start and end apart: 12 -> 10, of which waited for: 12 -> 8; matrix products, arithmetic and copies ran while one was open for 2% -> 6% of each run, Pallas kernels for 0% -> 0%
where the time goes in v1:
time: 651 us
  waiting for transfers between devices  459 us (71%)
  blocking collectives  71.2 us (11%)
  matrix products  58.6 us (9%)
  local copies, waits for them, and re-layouts  44.4 us (7%)
  between operations  15 us (2%)
    reduce_scatter x2, waiting for transfers between devices, solve_terms(): lax.psum_scatter(jnp.einsum('ski,kij->skj', right_rows, inverse, precisio...  152 us
    psum x2, waiting for transfers between devices, finish_level(): summed = lax.psum(partial_value, 'col')  124 us
    unnamed x11, waiting for transfers between devices  103 us
    all_to_all x2, blocking collectives, lax.all_to_all(jnp.stack([raw for _ in range(lax.axis_size('wide'))], axi...  71.2 us
    dot_general x3, matrix products, solve_terms(): jnp.einsum('ski,kij->skj', right_rows, inverse, precision=PRECISE, prefer...  50.4 us
    all_gather x2, waiting for transfers between devices, spread_solved(): gathered = lax.all_gather(solved_local, 'col', axis=2, tiled=True)  49.3 us
    all_gather x3, waiting for transfers between devices, spread_rhs(): return lax.all_gather(local_part, 'col', axis=0, tiled=True)  29.4 us
  transfers between devices with their start and end apart: 10, of which 8 were waited for; matrix products, arithmetic and copies ran while one was open for 6% of the time, Pallas kernels for 0%

profile of v1, /device:TPU:0, one launch (start us, length us, event | category | flops | bytes accessed | tf_op | source)
XLA Modules:
  0.0 650.6 jit_solution(3044809773003770590)
XLA Ops:
  8.0 29.4 %all-gather.15.cloned.1.call-done = f32[512,1024]{1,0:T(8,128)} async-done(((f32[64,1024]{1,0:T(8,128)}), f32[512,1024]{1,0:T(8,128)}) %all-gather.15.cloned.1.call-update) | async-done | bytes 2097168 | tf_op jit(solution)/shard_map/all_gather | solution.py:27
  37.4 30.4 %convolution_bitcast_fusion = f32[512,1,2048]{0,2,1:T(8,128)} fusion(f32[1024,2048]{1,0:T(8,128)} %param.13, f32[512,1024]{1,0:T(8,128)} %all-gather.15.cloned.1.call-done), kind=kOutput, calls=%fused_computation.3 | convolution fusion | flops 12884901888 | bytes 14680064 | tf_op jit(solution)/shard_map/ski,kij->skj/dot_general | solution.py:32
  67.8 11.0 %copy.79 = f32[512,1,2048]{2,1,0:T(1,128)} copy(f32[512,1,2048]{0,2,1:T(8,128)} %convolution_bitcast_fusion) | data formatting | bytes 8388608 | tf_op jit(solution)/shard_map/ski,kij->skj/transpose | solution.py:32
  80.7 102.3 %all-reduce.9.cloned.1.call-done = f32[512,1,2048]{2,1,0:T(1,128)} async-done(((f32[512,1,2048]{2,1,0:T(1,128)}), f32[512,1,2048]{2,1,0:T(1,128)}) %all-reduce.9.cloned.1.call-update) | async-done | bytes 4194320
  183.0 1.7 constant_dynamic-slice_fusion
  184.7 0.8 copy.80
  185.8 24.3 %all-gather.9.cloned.1.call-done = f32[32,1,16384]{2,1,0:T(1,128)} async-done(((f32[32,1,2048]{2,1,0:T(1,128)}), f32[32,1,16384]{2,1,0:T(1,128)}) %all-gather.9.cloned.1.call-update) | async-done | bytes 2097168 | tf_op jit(solution)/shard_map/all_gather | solution.py:46
  210.1 4.2 copy.81
  214.2 2.1 gather_fusion
  216.9 35.6 %all_to_all.10 = f32[16,32,2,512]{3,1,2,0:T(8,128)S(1)} all-to-all(f32[16,32,2,512]{3,1,2,0:T(8,128)S(1)} %stack.6), channel_id=1, replica_groups=mesh['wide'=16,'col'=8] {'wide'}, dimensions={0} | all-to-all | bytes 4194304 | tf_op jit(solution)/shard_map/all_to_all | solution.py:9
  252.7 1.4 copy-done.3
  254.1 4.8 convolution_bitcast_fusion.4
  259.0 62.1 %all-reduce.5.cloned.1.call-done = f32[512,2,512]{2,0,1:T(8,128)} async-done(((f32[512,2,512]{2,0,1:T(8,128)}), f32[512,2,512]{2,0,1:T(8,128)}) %all-reduce.5.cloned.1.call-update) | async-done | bytes 2097168 | tf_op jit(solution)/shard_map/psum | solution.py:55
  321.1 12.2 %convolution_bitcast_fusion.2 = f32[512,2,1024]{2,0,1:T(8,128)} fusion(f32[2,512,1024]{2,1,0:T(8,128)} %param.14, f32[512,2,512]{2,0,1:T(8,128)} %all-gather.7.cloned.1.call-done, f32[512,2,512]{2,0,1:T(8,128)} %all-reduce.5.cloned.1.call-done), kind=kOutput, calls=%fused_computation.5 | convolution fusion | flops 6442975232 | bytes 12582912 | tf_op jit(solution)/shard_map/ski,kij->skj/dot_general | solution.py:32
  333.4 77.5 %reduce-scatter.3.cloned.1.call-done = f32[32,2,1024]{2,0,1:T(8,128)} async-done(((f32[512,2,1024]{2,0,1:T(8,128)}), f32[32,2,1024]{2,0,1:T(8,128)}) %reduce-scatter.3.cloned.1.call-update) | async-done | bytes 262160 | tf_op jit(solution)/shard_map/reduce_scatter | solution.py:31
  411.0 0.8 copy.85
  412.1 25.0 %all-gather.13.cloned.1.call-done = f32[32,2,8192]{2,0,1:T(8,128)} async-done(((f32[32,2,1024]{2,0,1:T(8,128)}), f32[32,2,8192]{2,0,1:T(8,128)}) %all-gather.13.cloned.1.call-update) | async-done | bytes 2097168 | tf_op jit(solution)/shard_map/all_gather | solution.py:46
  437.1 4.5 copy.86
  441.6 4.0 concatenate.6
  445.6 3.0 copy.88
  448.6 2.4 pad_maximum_fusion
  451.0 2.7 gather_fusion.1
  454.2 35.6 %all_to_all.11 = f32[16,32,4,256]{3,1,2,0:T(8,128)S(1)} all-to-all(f32[16,32,4,256]{3,1,2,0:T(8,128)S(1)} %stack.7), channel_id=1, replica_groups=mesh['wide'=16,'col'=8] {'wide'}, dimensions={0} | all-to-all | bytes 4194304 | tf_op jit(solution)/shard_map/all_to_all | solution.py:9
  490.1 1.0 copy-done.4
  491.0 3.3 convolution_bitcast_fusion.3
  494.5 62.1 %all-reduce.7.cloned.1.call-done = f32[512,4,256]{2,0,1:T(8,128)} async-done(((f32[512,4,256]{2,0,1:T(8,128)}), f32[512,4,256]{2,0,1:T(8,128)}) %all-reduce.7.cloned.1.call-update) | async-done | bytes 2097168 | tf_op jit(solution)/shard_map/psum | solution.py:55
  556.6 7.7 %convolution_bitcast_fusion.1 = f32[512,4,512]{2,0,1:T(8,128)} fusion(f32[4,256,512]{2,1,0:T(8,128)S(1)} %copy-done, f32[512,4,256]{2,0,1:T(8,128)} %all-gather.11.cloned.1.call-done, f32[512,4,256]{2,0,1:T(8,128)} %all-reduce.7.cloned.1.call-done), kind=kOutput, calls=%fused_computation.4 | convolution fusion | flops 3221749760 | bytes 10485760 | tf_op jit(solution)/shard_map/ski,kij->skj/dot_general | solution.py:32
  564.4 0.9 copy-done.2
  565.3 0.8 copy.99
  566.1 0.9 copy.93
  567.0 75.0 %reduce-scatter.5.cloned.1.call-done = f32[32,4,512]{2,0,1:T(8,128)} async-done(((f32[512,4,512]{2,0,1:T(8,128)}), f32[32,4,512]{2,0,1:T(8,128)}) %reduce-scatter.5.cloned.1.call-update) | async-done | bytes 262160 | tf_op jit(solution)/shard_map/reduce_scatter | solution.py:31
  642.0 1.8 copy.94
  (66 shorter events, 4.3 us)
Async XLA Ops:
  7.2 549.4 %copy-start = (f32[4,256,512]{2,1,0:T(8,128)S(1)}, f32[4,256,512]{2,1,0:T(8,128)}, u32[]{:S(2)}) copy-start(f32[4,256,512]{2,1,0:T(8,128)} %param.15) | copy-start | bytes 6291460
  7.2 30.2 %all-gather.15.cloned.1.call-start = ((), (), s32[]{:S(2)}) async-start(), calls=%async_computation.12 | async-start | bytes 2359296 | tf_op jit(solution)/shard_map/all_gather | solution.py:27
  7.9 175.1 %all-reduce.9.cloned.1.call-start = ((), (), s32[]{:S(2)}) async-start(), calls=%async_computation.13 | async-start | bytes 8388608
  78.8 0.7 copy-start.10
  78.8 105.9 %copy-start.6 = (f32[64,2,512]{2,1,0:T(2,128)S(1)}, f32[64,2,512]{2,1,0:T(2,128)}, u32[]{:S(2)}) copy-start(f32[64,2,512]{2,1,0:T(2,128)} %param.11) | copy-start | bytes 786436
  78.8 106.7 %copy-start.9 = (s32[2,4]{1,0:T(2,128)S(1)}, s32[2,4]{1,0:T(2,128)}, u32[]{:S(2)}) copy-start(s32[2,4]{1,0:T(2,128)} %param.18) | copy-start | bytes 100
  78.9 131.2 %all-gather.9.cloned.1.call-start = ((), (), s32[]{:S(2)}) async-start(), calls=%async_computation.5 | async-start | bytes 2359296 | tf_op jit(solution)/shard_map/all_gather | solution.py:46
  184.7 74.3 %all-gather.7.cloned.1.call-start = ((), (), s32[]{:S(2)}) async-start(), calls=%async_computation.4 | async-start | bytes 2359296 | tf_op jit(solution)/shard_map/all_gather | solution.py:27
  185.5 135.6 %all-reduce.5.cloned.1.call-start = ((), (), s32[]{:S(2)}) async-start(), calls=%async_computation.6 | async-start | bytes 4194304 | tf_op jit(solution)/shard_map/psum | solution.py:55
  252.5 1.6 copy-start.3
  258.9 152.0 %reduce-scatter.3.cloned.1.call-start = ((), (), s32[]{:S(2)}) async-start(), calls=%async_computation.7 | async-start | bytes 4456448 | tf_op jit(solution)/shard_map/reduce_scatter | solution.py:31
  333.3 77.7 %copy-start.7 = (f32[64,4,256]{2,1,0:T(4,128)S(1)}, f32[64,4,256]{2,1,0:T(4,128)}, u32[]{:S(2)}) copy-start(f32[64,4,256]{2,1,0:T(4,128)} %param.12) | copy-start | bytes 786436
  333.3 78.5 %copy-start.8 = (s32[4,2]{0,1:T(2,128)S(1)}, s32[4,2]{0,1:T(2,128)}, u32[]{:S(2)}) copy-start(s32[4,2]{0,1:T(2,128)} %param.19) | copy-start | bytes 100
  333.4 103.8 %all-gather.13.cloned.1.call-start = ((), (), s32[]{:S(2)}) async-start(), calls=%async_computation.9 | async-start | bytes 2359296 | tf_op jit(solution)/shard_map/all_gather | solution.py:46
  410.9 83.5 %all-gather.11.cloned.1.call-start = ((), (), s32[]{:S(2)}) async-start(), calls=%async_computation.8 | async-start | bytes 2359296 | tf_op jit(solution)/shard_map/all_gather | solution.py:27
  411.8 144.8 %all-reduce.7.cloned.1.call-start = ((), (), s32[]{:S(2)}) async-start(), calls=%async_computation.10 | async-start | bytes 4194304 | tf_op jit(solution)/shard_map/psum | solution.py:55
  445.6 3.0 copy-start.1
  489.8 1.2 copy-start.4
  494.4 147.6 %reduce-scatter.5.cloned.1.call-start = ((), (), s32[]{:S(2)}) async-start(), calls=%async_computation.11 | async-start | bytes 4456448 | tf_op jit(solution)/shard_map/reduce_scatter | solution.py:31
  564.4 0.9 copy-start.2
  564.4 1.7 copy-start.5
Sparse Core Ops, SparseCore 0:
  9.7 27.5 all-gather.14
  79.0 103.9 all-reduce.8
  185.2 24.7 all-gather.8
  212.2 25.4 all-gather.6
  259.1 62.0 all-reduce.4
  333.5 77.3 reduce-scatter.2
  412.7 24.3 all-gather.12
  439.5 25.4 all-gather.10
  494.5 62.0 all-reduce.6
  564.5 77.4 reduce-scatter.4
